TPU v7x, 256 devices: a whole 4x4x8 slice. The times are simulated.
256 devices in a mesh: seq: 64 (over y, z, core), ch: 4 (over x).
Axes of the slice: x: 4, y: 4, z: 8, core: 2. Of those that a mesh axis runs over, the one named last changes fastest.
Arguments:
- query_stream: bfloat16 [16384, 4096], P('seq', 'ch'), may hold values from -16 to 16
- key_stream: bfloat16 [16384, 4096], P('seq', 'ch'), may hold values from -6 to 6
- value_stream: bfloat16 [16384, 4096], P('seq', 'ch'), may hold values from -6 to 6
- filter_taps: float32 [4096, 128], P('ch'), may hold values from -0.5 to 0.5
- out_weight: bfloat16 [4096, 4096], P('seq', 'ch'), may hold values from -0.09375 to 0.09375
- upstream: bfloat16 [16384, 4096], P('seq', 'ch'), may hold values from -6 to 6
Outputs:
- mixed: bfloat16 [16384, 4096], P('seq', 'ch')
- grad_query: bfloat16 [16384, 4096], P('seq', 'ch')
- grad_key: bfloat16 [16384, 4096], P('seq', 'ch')
- grad_value: bfloat16 [16384, 4096], P('seq', 'ch')
- grad_filter: float32 [4096, 128], P('ch')
- grad_weight: float32 [4096, 4096], P('seq', 'ch')
All inputs are finite; a program needn't handle non-finite values.
Results may differ from a plain program's by a relative error of at most 0.0057.
Values may be sent and summed in bfloat16 or wider, within the bound.
No kernel may reach another device: no remote copies, remote signals or barrier semaphores. Data moves between devices by JAX's collectives and lax.ppermute only.
A program may use at most 128 MiB of HBM per device.

v0:
```python
import jax
import jax.numpy as jnp
from jax import lax
from jax.sharding import Mesh
from jax.sharding import PartitionSpec as P

SUB = ("sy", "sz", "sc")


def seq_factors(mesh):
    count = mesh.shape["seq"]
    try:
        devices = list(mesh.devices[:, 0])
        cores = len({d.core_on_chip for d in devices})
        zs = len({d.coords[2] for d in devices})
        if cores * zs and count % (cores * zs) == 0:
            return (count // (cores * zs), zs, cores)
    except Exception:
        pass
    return (count // 16, 8, 2) if count % 16 == 0 else (1, 1, count)


def from_behind(value, axis, count, steps):
    initial, last = (max(0, -steps), min(count, count - steps))
    return lax.ppermute(value, axis, [(source, source + steps) for source in range(initial, last)])


def depthwise(signal, kernel):
    output = lax.conv_general_dilated(
        signal[None],
        kernel[:, None, :],
        (1,),
        "VALID",
        dimension_numbers=("NWC", "WIO", "NWC"),
        feature_group_count=signal.shape[1],
        precision=lax.Precision.HIGHEST,
    )
    return output[0]


def gather_ch(part, count):
    here = lax.axis_index("ch")
    pieces = [part] + [
        lax.ppermute(part, "ch", [(i, (i + k) % count) for i in range(count)])
        for k in range(1, count)
    ]
    stacked = jnp.stack(pieces)[(here - jnp.arange(count)) % count]
    return jnp.concatenate([stacked[j] for j in range(count)], axis=1)


def scatter_ch(whole, count):
    here = lax.axis_index("ch")
    width = whole.shape[1] // count
    total = lax.dynamic_slice_in_dim(whole, here * width, width, 1)
    for k in range(1, count):
        block = lax.dynamic_slice_in_dim(whole, (here + k) % count * width, width, 1)
        total = total + lax.ppermute(block, "ch", [(i, (i + k) % count) for i in range(count)])
    return total


def butterfly_sum(value, factors):
    for axis, size in zip(SUB, factors):
        bit = 1
        while bit < size:
            value = value + lax.ppermute(value, axis, [(i, i ^ bit) for i in range(size)])
            bit *= 2
    return value


def make_body(factors, chs):
    n_seq = factors[0] * factors[1] * factors[2]

    def body(query_stream, key_stream, value_stream, filter_taps, out_weight, upstream):
        rows_here = query_stream.shape[0]
        tap_count = filter_taps.shape[1]
        keyed = (key_stream.astype(jnp.float32) * value_stream.astype(jnp.float32)).astype(
            jnp.bfloat16
        )
        rim_before = from_behind(keyed[rows_here - (tap_count - 1) :], SUB, n_seq, 1)
        front_pad = jnp.concatenate([rim_before, keyed], axis=0).astype(jnp.float32)
        response = depthwise(front_pad, filter_taps.T[::-1])
        query_wide = query_stream.astype(jnp.float32)
        gated = (query_wide * response).astype(jnp.bfloat16)
        gated_full = gather_ch(gated, chs)
        weight_cols = lax.all_gather(out_weight, SUB, axis=0, tiled=True)
        mixed = jnp.dot(gated_full, weight_cols, preferred_element_type=jnp.float32).astype(
            jnp.bfloat16
        )
        partial_terms = lax.dot_general(
            upstream, weight_cols, (((1,), (1,)), ((), ())), preferred_element_type=jnp.float32
        )
        grad_gated = scatter_ch(partial_terms, chs)
        grad_query = (grad_gated * response).astype(jnp.bfloat16)
        grad_response = grad_gated * query_wide
        rim_after = from_behind(grad_response[: tap_count - 1], SUB, n_seq, -1)
        back_pad = jnp.concatenate([grad_response, rim_after], axis=0)
        grad_keyed = depthwise(back_pad, filter_taps.T)
        grad_key = (grad_keyed * value_stream.astype(jnp.float32)).astype(jnp.bfloat16)
        grad_value = (grad_keyed * key_stream.astype(jnp.float32)).astype(jnp.bfloat16)
        filter_local = depthwise(front_pad, grad_response)[::-1].T
        grad_filter = butterfly_sum(filter_local, factors)
        block = out_weight.shape[0]
        columns = lax.slice_in_dim(gated_full, 0, n_seq * block, axis=1)
        columns = columns.reshape((rows_here,) + factors + (block,)).transpose(0, 3, 2, 1, 4)
        columns = columns.reshape(rows_here, n_seq * block)
        partial = lax.dot_general(
            columns, upstream, (((0,), (0,)), ((), ())), preferred_element_type=jnp.float32
        )
        for axis in ("sc", "sz", "sy"):
            partial = lax.psum_scatter(partial, axis, scatter_dimension=0, tiled=True)
        return (mixed, grad_query, grad_key, grad_value, grad_filter, partial)

    return body


def solution(mesh):
    factors = seq_factors(mesh)
    chs = mesh.shape["ch"]
    fine = Mesh(mesh.devices.reshape(factors + (chs,)), SUB + ("ch",))
    rows = P(SUB, "ch")
    in_specs = (rows, rows, rows, P("ch", None), rows, rows)
    out_specs = (rows, rows, rows, rows, P("ch", None), rows)
    return jax.shard_map(
        make_body(factors, chs), mesh=fine, in_specs=in_specs, out_specs=out_specs, check_vma=False
    )
```

profile of v0, /device:TPU:1, one launch (start us, length us, event | category | flops | bytes accessed | tf_op | source)
XLA Modules:
  0.0 451.6 jit_solution(6935114478768854161)
XLA Ops:
  8.0 90.0 %all-gather.2.cloned.1.call-done = bf16[4096,1024]{1,0:T(8,128)(2,1)} async-done(((bf16[64,1024]{1,0:T(8,128)(2,1)}), bf16[4096,1024]{1,0:T(8,128)(2,1)}) %all-gather.2.cloned.1.call-update) | async-done | bytes 8388624 | tf_op jit(solution)/shard_map/all_gather | solution.py:85
  98.0 5.7 %fusion.27 = f32[256,4096]{1,0:T(8,128)S(1)} fusion(bf16[256,1024]{1,0:T(8,128)(2,1)S(1)} %copy-done, bf16[4096,1024]{1,0:T(8,128)(2,1)} %all-gather.2.cloned.1.call-done), kind=kOutput, calls=%fused_computation.51 | convolution fusion | flops 2147483648 | bytes 13107200 | tf_op jit(solution)/shard_map/dot_general | solution.py:89
  110.9 21.7 %collective-permute-done.4 = f32[256,1024]{1,0:T(8,128)S(1)} collective-permute-done((f32[256,1024]{1,0:T(8,128)}, f32[256,1024]{1,0:T(8,128)S(1)}, u32[]{:S(2)}, u32[]{:S(2)}) %collective-permute-start.4) | collective-permute-done | bytes 1048608 | tf_op jit(solution)/shard_map/ppermute | solution.py:57
  133.5 22.5 %collective-permute-done.5 = f32[256,1024]{1,0:T(8,128)} collective-permute-done((f32[256,1024]{1,0:T(8,128)}, f32[256,1024]{1,0:T(8,128)}, u32[]{:S(2)}, u32[]{:S(2)}) %collective-permute-start.5) | collective-permute-done | bytes 1048608 | tf_op jit(solution)/shard_map/ppermute | solution.py:57
  156.1 3.7 convert_multiply_fusion.3
  159.8 3.0 collective-permute-start.7
  163.3 7.3 %collective-permute-done.7 = f32[127,1024]{1,0:T(8,128)} collective-permute-done((f32[127,1024]{1,0:T(8,128)S(1)}, f32[127,1024]{1,0:T(8,128)}, u32[]{:S(2)}, u32[]{:S(2)}) %collective-permute-start.7) | collective-permute-done | bytes 520224 | tf_op jit(solution)/shard_map/ppermute | solution.py:25
  171.9 10.6 %fusion.8 = f32[1,256,1024]{2,0,1:T(1,128)S(1)} fusion(f32[128,1,1024]{2,1,0:T(1,128)S(1)} %copy.20, f32[1,383,1024]{2,1,0:T(8,128)S(1)} %maximum_bitcast_fusion.1), kind=kOutput, calls=%fused_computation.12 | convolution fusion | flops 402653184 | bytes 3141632 | tf_op jit(solution)/shard_map/conv_general_dilated | solution.py:29
  189.4 10.6 %fusion.15 = f32[1,256,1024]{2,0,1:T(1,128)S(1)} fusion(f32[128,1,1024]{2,1,0:T(1,128)S(1)} %copy.18, bf16[1,383,1024]{2,1,0:T(8,128)(2,1)S(1)} %maximum_bitcast_fusion.2), kind=kOutput, calls=%fused_computation.22 | convolution fusion | flops 402653184 | bytes 2357248 | tf_op jit(solution)/shard_map/conv_general_dilated | solution.py:29
  204.0 20.9 %collective-permute-done.3 = bf16[256,1024]{1,0:T(8,128)(2,1)S(1)} collective-permute-done((bf16[256,1024]{1,0:T(8,128)(2,1)S(1)}, bf16[256,1024]{1,0:T(8,128)(2,1)S(1)}, u32[]{:S(2)}, u32[]{:S(2)}) %collective-permute-start.3) | collective-permute-done | bytes 524320 | tf_op jit(solution)/shard_map/ppermute | solution.py:44
  224.9 3.9 collective-permute-done.1
  230.4 2.3 gather_fusion
  238.2 8.1 %fusion.28 = f32[4096,1024]{1,0:T(8,128)} fusion(bf16[256,4096]{0,1:T(8,128)(2,1)S(1)} %bitcast.50, bf16[256,1024]{1,0:T(8,128)(2,1)S(1)} %copy-done), kind=kOutput, calls=%fused_computation.52 | convolution fusion | flops 2147483648 | bytes 19398656 | tf_op jit(solution)/shard_map/dot_general | solution.py:106
  246.4 27.5 %reduce-scatter.4.cloned.1.call-done = f32[2048,1024]{1,0:T(8,128)} async-done(((f32[4096,1024]{1,0:T(8,128)}), f32[2048,1024]{1,0:T(8,128)}) %reduce-scatter.4.cloned.1.call-update) | async-done | bytes 8388624 | tf_op jit(solution)/shard_map/reduce_scatter | solution.py:110
  275.4 10.6 %fusion.13 = f32[1,128,1024]{2,0,1:T(1,128)S(1)} fusion(bf16[1,383,1024]{2,1,0:T(8,128)(2,1)S(1)} %copy-done.12, f32[256,1,1024]{2,0,1:T(8,128)S(1)} %bitcast.51), kind=kOutput, calls=%fused_computation.20 | convolution fusion | flops 402653184 | bytes 2357248 | tf_op jit(solution)/shard_map/conv_general_dilated | solution.py:29
  287.4 12.3 %collective-permute-done.8 = f32[1024,128]{0,1:T(8,128)S(1)} collective-permute-done((f32[1024,128]{0,1:T(8,128)S(1)}, f32[1024,128]{0,1:T(8,128)S(1)}, u32[]{:S(2)}, u32[]{:S(2)}) %collective-permute-start.8) | collective-permute-done | bytes 524320 | tf_op jit(solution)/shard_map/ppermute | solution.py:65
  299.8 2.5 collective-permute-start.9
  302.3 11.4 %collective-permute-done.9 = f32[1024,128]{0,1:T(8,128)S(1)} collective-permute-done((f32[1024,128]{0,1:T(8,128)S(1)}, f32[1024,128]{0,1:T(8,128)S(1)}, u32[]{:S(2)}, u32[]{:S(2)}) %collective-permute-start.9) | collective-permute-done | bytes 524320 | tf_op jit(solution)/shard_map/ppermute | solution.py:65
  314.9 66.7 %reduce-scatter.6.cloned.1.call-done = f32[256,1024]{1,0:T(8,128)} async-done(((f32[2048,1024]{1,0:T(8,128)}), f32[256,1024]{1,0:T(8,128)}) %reduce-scatter.6.cloned.1.call-update) | async-done | bytes 1048592 | tf_op jit(solution)/shard_map/reduce_scatter | solution.py:110
  381.7 2.4 collective-permute-start.11
  384.1 23.5 %collective-permute-done.11 = f32[1024,128]{0,1:T(8,128)S(1)} collective-permute-done((f32[1024,128]{0,1:T(8,128)S(1)}, f32[1024,128]{0,1:T(8,128)S(1)}, u32[]{:S(2)}, u32[]{:S(2)}) %collective-permute-start.11) | collective-permute-done | bytes 524320 | tf_op jit(solution)/shard_map/ppermute | solution.py:65
  407.7 4.0 collective-permute-start.12
  411.7 24.2 %collective-permute-done.12 = f32[1024,128]{0,1:T(8,128)S(1)} collective-permute-done((f32[1024,128]{0,1:T(8,128)S(1)}, f32[1024,128]{0,1:T(8,128)S(1)}, u32[]{:S(2)}, u32[]{:S(2)}) %collective-permute-start.12) | collective-permute-done | bytes 524320 | tf_op jit(solution)/shard_map/ppermute | solution.py:65
  437.4 6.6 %fusion.10 = bf16[256,1024]{1,0:T(8,128)(2,1)} fusion(bf16[4096,1024]{1,0:T(8,128)(2,1)} %all-gather.2.cloned.1.call-done, bf16[256,1024]{1,0:T(8,128)(2,1)S(1)} %copy-done.18, bf16[256,1024]{1,0:T(8,128)(2,1)S(1)} %copy-done.17, bf16[256,1024]{1,0:T(8,128)(2,1)S(1)} %copy-done.16, bf16[256,1024]{1,0:T(8,128)(2,1)S(1)} %copy-done.15), kind=kOutput, calls=%fused_computation.19 | convolution fusion | flops 2156134400 | bytes 11010048 | tf_op jit(solution)/shard_map/dot_general | solution.py:86
  (91 shorter events, 35.1 us)
Async XLA Ops:
  7.2 90.8 %copy-start = (bf16[256,1024]{1,0:T(8,128)(2,1)S(1)}, bf16[256,1024]{1,0:T(8,128)(2,1)}, u32[]{:S(2)}) copy-start(bf16[256,1024]{1,0:T(8,128)(2,1)} %param.11) | copy-start | bytes 1572868
  7.2 90.8 %all-gather.2.cloned.1.call-start = ((), (), s32[]{:S(2)}) async-start(), calls=%async_computation.3 | async-start | bytes 8519680 | tf_op jit(solution)/shard_map/all_gather | solution.py:85
  7.9 266.0 %reduce-scatter.4.cloned.1.call-start = ((), (), s32[]{:S(2)}) async-start(), calls=%async_computation.4 | async-start | bytes 25165824 | tf_op jit(solution)/shard_map/reduce_scatter | solution.py:110
  103.8 52.3 %copy-start.8 = (bf16[256,1024]{1,0:T(8,128)(2,1)S(1)}, bf16[256,1024]{1,0:T(8,128)(2,1)}, u32[]{:S(2)}) copy-start(bf16[256,1024]{1,0:T(8,128)(2,1)} %param.6) | copy-start | bytes 1572868
  106.7 25.9 %collective-permute-start.4 = (f32[256,1024]{1,0:T(8,128)}, f32[256,1024]{1,0:T(8,128)S(1)}, u32[]{:S(2)}, u32[]{:S(2)}) collective-permute-start(f32[256,1024]{1,0:T(8,128)} %get-tuple-element.20), channel_id=1, source_target_pairs={{0,1},{1,2},{2,3},{3,0},{4,5},{5,6},{6,7},{7,4},{8,9},{9,10},{10,1... | collective-permute-start | bytes 3145736 | tf_op jit(solution)/shard_map/ppermute | solution.py:57
  107.9 24.7 %collective-permute-start.6 = (f32[256,1024]{1,0:T(8,128)}, f32[256,1024]{1,0:T(8,128)}, u32[]{:S(2)}, u32[]{:S(2)}) collective-permute-start(f32[256,1024]{1,0:T(8,128)} %get-tuple-element.21), channel_id=1, source_target_pairs={{0,3},{1,0},{2,1},{3,2},{4,7},{5,4},{6,5},{7,6},{8,11},{9,8},{10,9... | collective-permute-start | bytes 3145736 | tf_op jit(solution)/shard_map/ppermute | solution.py:57
  109.4 46.7 %collective-permute-start.5 = (f32[256,1024]{1,0:T(8,128)}, f32[256,1024]{1,0:T(8,128)}, u32[]{:S(2)}, u32[]{:S(2)}) collective-permute-start(f32[256,1024]{1,0:T(8,128)} %get-tuple-element.22), channel_id=1, source_target_pairs={{0,2},{1,3},{2,0},{3,1},{4,6},{5,7},{6,4},{7,5},{8,10},{9,11},{10,... | collective-permute-start | bytes 3145736 | tf_op jit(solution)/shard_map/ppermute | solution.py:57
  159.8 10.8 %collective-permute-start.7 = (f32[127,1024]{1,0:T(8,128)S(1)}, f32[127,1024]{1,0:T(8,128)}, u32[]{:S(2)}, u32[]{:S(2)}) collective-permute-start(f32[127,1024]{1,0:T(8,128)S(1)} %slice.31), channel_id=1, source_target_pairs={{4,0},{8,4},{12,8},{16,12},{20,16},{24,20},{28,24},{32,28},{36,32}... | collective-permute-start | bytes 1560584 | tf_op jit(solution)/shard_map/ppermute | solution.py:25
  184.0 5.2 %collective-permute-start = (bf16[127,1024]{1,0:T(8,128)(2,1)S(1)}, bf16[127,1024]{1,0:T(8,128)(2,1)S(1)}, u32[]{:S(2)}, u32[]{:S(2)}) collective-permute-start(bf16[127,1024]{1,0:T(8,128)(2,1)S(1)} %slice.26), channel_id=1, source_target_pairs={{0,4},{4,8},{8,12},{12,16},{16,20},{20,24},{24,28},{28,32},{32,36}... | collective-permute-start | bytes 780296 | tf_op jit(solution)/shard_map/ppermute | solution.py:25
  201.3 23.6 %collective-permute-start.3 = (bf16[256,1024]{1,0:T(8,128)(2,1)S(1)}, bf16[256,1024]{1,0:T(8,128)(2,1)S(1)}, u32[]{:S(2)}, u32[]{:S(2)}) collective-permute-start(bf16[256,1024]{1,0:T(8,128)(2,1)S(1)} %get-tuple-element.35), channel_id=1, source_target_pairs={{0,3},{1,0},{2,1},{3,2},{4,7},{5,4},{6,5},{7,6},{8,11},{9,8},{10,9... | collective-permute-start | bytes 1572872 | tf_op jit(solution)/shard_map/ppermute | solution.py:44
  203.1 21.8 %collective-permute-start.2 = (bf16[256,1024]{1,0:T(8,128)(2,1)S(1)}, bf16[256,1024]{1,0:T(8,128)(2,1)S(1)}, u32[]{:S(2)}, u32[]{:S(2)}) collective-permute-start(bf16[256,1024]{1,0:T(8,128)(2,1)S(1)} %get-tuple-element.35), channel_id=1, source_target_pairs={{0,2},{1,3},{2,0},{3,1},{4,6},{5,7},{6,4},{7,5},{8,10},{9,11},{10,... | collective-permute-start | bytes 1572872 | tf_op jit(solution)/shard_map/ppermute | solution.py:44
  204.0 24.9 %collective-permute-start.1 = (bf16[256,1024]{1,0:T(8,128)(2,1)S(1)}, bf16[256,1024]{1,0:T(8,128)(2,1)S(1)}, u32[]{:S(2)}, u32[]{:S(2)}) collective-permute-start(bf16[256,1024]{1,0:T(8,128)(2,1)S(1)} %get-tuple-element.35), channel_id=1, source_target_pairs={{0,1},{1,2},{2,3},{3,0},{4,5},{5,6},{6,7},{7,4},{8,9},{9,10},{10,1... | collective-permute-start | bytes 1572872 | tf_op jit(solution)/shard_map/ppermute | solution.py:44
  246.4 135.2 %reduce-scatter.6.cloned.1.call-start = ((), (), s32[]{:S(2)}) async-start(), calls=%async_computation.5 | async-start | bytes 9437184 | tf_op jit(solution)/shard_map/reduce_scatter | solution.py:110
  274.0 171.1 %reduce-scatter.8.cloned.1.call-start = ((), (), s32[]{:S(2)}) async-start(), calls=%async_computation.6 | async-start | bytes 1310720 | tf_op jit(solution)/shard_map/reduce_scatter | solution.py:110
  286.4 13.3 %collective-permute-start.8 = (f32[1024,128]{0,1:T(8,128)S(1)}, f32[1024,128]{0,1:T(8,128)S(1)}, u32[]{:S(2)}, u32[]{:S(2)}) collective-permute-start(f32[1024,128]{0,1:T(8,128)S(1)} %bitcast.52), channel_id=1, source_target_pairs={{0,64},{64,0},{128,192},{192,128},{1,65},{65,1},{129,193},{193,129... | collective-permute-start | bytes 1572872 | tf_op jit(solution)/shard_map/ppermute | solution.py:65
  299.8 14.0 %collective-permute-start.9 = (f32[1024,128]{0,1:T(8,128)S(1)}, f32[1024,128]{0,1:T(8,128)S(1)}, u32[]{:S(2)}, u32[]{:S(2)}) collective-permute-start(f32[1024,128]{0,1:T(8,128)S(1)} %bitcast_add_fusion), channel_id=1, source_target_pairs={{0,128},{64,192},{128,0},{192,64},{1,129},{65,193},{129,1},{193,65... | collective-permute-start | bytes 1572872 | tf_op jit(solution)/shard_map/ppermute | solution.py:65
  313.8 67.8 %collective-permute-start.10 = (f32[1024,128]{0,1:T(8,128)S(1)}, f32[1024,128]{0,1:T(8,128)S(1)}, u32[]{:S(2)}, u32[]{:S(2)}) collective-permute-start(f32[1024,128]{0,1:T(8,128)S(1)} %add.103), channel_id=1, source_target_pairs={{0,8},{8,0},{16,24},{24,16},{32,40},{40,32},{48,56},{56,48},{1,9},... | collective-permute-start | bytes 1572872 | tf_op jit(solution)/shard_map/ppermute | solution.py:65
  381.6 55.8 %copy-start.15 = (bf16[256,1024]{1,0:T(8,128)(2,1)S(1)}, bf16[256,1024]{1,0:T(8,128)(2,1)}, u32[]{:S(2)}) copy-start(bf16[256,1024]{1,0:T(8,128)(2,1)} %get-tuple-element.24) | copy-start | bytes 1572868
  381.6 55.8 %copy-start.16 = (bf16[256,1024]{1,0:T(8,128)(2,1)S(1)}, bf16[256,1024]{1,0:T(8,128)(2,1)}, u32[]{:S(2)}) copy-start(bf16[256,1024]{1,0:T(8,128)(2,1)} %get-tuple-element.25) | copy-start | bytes 1572868
  381.6 55.8 %copy-start.17 = (bf16[256,1024]{1,0:T(8,128)(2,1)S(1)}, bf16[256,1024]{1,0:T(8,128)(2,1)}, u32[]{:S(2)}) copy-start(bf16[256,1024]{1,0:T(8,128)(2,1)} %get-tuple-element.26) | copy-start | bytes 1572868
  381.6 55.8 %copy-start.18 = (bf16[256,1024]{1,0:T(8,128)(2,1)S(1)}, bf16[256,1024]{1,0:T(8,128)(2,1)}, u32[]{:S(2)}) copy-start(bf16[256,1024]{1,0:T(8,128)(2,1)} %get-tuple-element.27) | copy-start | bytes 1572868
  381.7 25.9 %collective-permute-start.11 = (f32[1024,128]{0,1:T(8,128)S(1)}, f32[1024,128]{0,1:T(8,128)S(1)}, u32[]{:S(2)}, u32[]{:S(2)}) collective-permute-start(f32[1024,128]{0,1:T(8,128)S(1)} %add.104), channel_id=1, source_target_pairs={{0,16},{8,24},{16,0},{24,8},{32,48},{40,56},{48,32},{56,40},{1,17}... | collective-permute-start | bytes 1572872 | tf_op jit(solution)/shard_map/ppermute | solution.py:65
  407.7 28.2 %collective-permute-start.12 = (f32[1024,128]{0,1:T(8,128)S(1)}, f32[1024,128]{0,1:T(8,128)S(1)}, u32[]{:S(2)}, u32[]{:S(2)}) collective-permute-start(f32[1024,128]{0,1:T(8,128)S(1)} %add.105), channel_id=1, source_target_pairs={{0,32},{8,40},{16,48},{24,56},{32,0},{40,8},{48,16},{56,24},{1,33}... | collective-permute-start | bytes 1572872 | tf_op jit(solution)/shard_map/ppermute | solution.py:65
  436.0 8.0 %collective-permute-start.13 = (f32[1024,128]{0,1:T(8,128)S(1)}, f32[1024,128]{0,1:T(8,128)S(1)}, u32[]{:S(2)}, u32[]{:S(2)}) collective-permute-start(f32[1024,128]{0,1:T(8,128)S(1)} %add.106), channel_id=1, source_target_pairs={{0,4},{4,0},{1,5},{5,1},{2,6},{6,2},{3,7},{7,3},{8,12},{12,8},{9,1... | collective-permute-start | bytes 1572872 | tf_op jit(solution)/shard_map/ppermute | solution.py:65
  (13 other events, 129.9 us)
Sparse Core Ops, SparseCore 0:
  10.8 87.1 all-gather.1
  246.5 27.4 reduce-scatter.3
  276.5 105.0 reduce-scatter.5
  384.6 25.2 reduce-scatter.7
where the time goes:
time: 452 us
  waiting for transfers between devices  335 us (74%)
  matrix products  52.3 us (12%)
  starting transfers between devices  24.4 us (5%)
  local copies, waits for them, and re-layouts  15.8 us (3%)
  between operations  14.2 us (3%)
  other arithmetic  10 us (2%)
    reduce_scatter x3, waiting for transfers between devices, body(): partial = lax.psum_scatter(partial, axis, scatter_dimension=0, tiled=True)  94.2 us
    all_gather x1, waiting for transfers between devices, body(): weight_cols = lax.all_gather(out_weight, SUB, axis=0, tiled=True)  90 us
    ppermute x6, waiting for transfers between devices, butterfly_sum(): lax.ppermute(value, axis, [(i, i ^ bit) for i in range(size)])  71.4 us
    ppermute x3, waiting for transfers between devices, scatter_ch(): lax.ppermute(block, 'ch', [(i, (i + k) % count) for i in range(count)])  44.2 us
    conv_general_dilated x3, matrix products, depthwise(): lax.conv_general_dilated(signal[None], kernel[:, None, :], (1,), 'VALID',...  31.8 us
    ppermute x3, waiting for transfers between devices, gather_ch(): lax.ppermute(part, 'ch', [(i, (i + k) % count) for i in range(count)])  24.8 us
    ppermute x6, starting transfers between devices, butterfly_sum(): lax.ppermute(value, axis, [(i, i ^ bit) for i in range(size)])  12.5 us
    ppermute x2, waiting for transfers between devices, from_behind(): lax.ppermute(value, axis, [(source, source + steps) for source in range(i...  9.48 us
  transfers between devices with their start and end apart: 18, of which 13 were waited for; matrix products, arithmetic and copies ran while one was open for 5% of the time, Pallas kernels for 0%

commit v1 on v0

--- a/solution.py
+++ b/solution.py
@@ -82,7 +82,9 @@
         query_wide = query_stream.astype(jnp.float32)
         gated = (query_wide * response).astype(jnp.bfloat16)
         gated_full = gather_ch(gated, chs)
-        weight_cols = lax.all_gather(out_weight, SUB, axis=0, tiled=True)
+        weight_cols = jnp.concatenate(
+            lax.all_to_all(jnp.stack([out_weight] * lax.axis_size(SUB)), SUB, 0, 0), axis=0
+        )
         mixed = jnp.dot(gated_full, weight_cols, preferred_element_type=jnp.float32).astype(
             jnp.bfloat16
         )

time: 452 us -> 565 us (1.25)
  waiting for transfers between devices: 335 us -> 430 us
  starting transfers between devices: 24.4 us -> 36.8 us
    all_to_all x0 -> x1, waiting for transfers between devices: none -> 186 us  [body(): lax.all_to_all(jnp.stack([out_weight] * lax.axis_size(SUB)), SUB, 0, 0)]
    all_gather x1 -> x0, waiting for transfers between devices: 90 us -> none  [body(): weight_cols = lax.all_gather(out_weight, SUB, axis=0, tiled=True)]
    all_to_all x0 -> x1, starting transfers between devices: none -> 13.3 us  [body(): lax.all_to_all(jnp.stack([out_weight] * lax.axis_size(SUB)), SUB, 0, 0)]
  transfers between devices with their start and end apart: 18 -> 18, of which waited for: 13 -> 14; matrix products, arithmetic and copies ran while one was open for 5% -> 4% of each run, Pallas kernels for 0% -> 0%
where the time goes in v1:
time: 565 us
  waiting for transfers between devices  430 us (76%)
  matrix products  52.2 us (9%)
  starting transfers between devices  36.8 us (7%)
  local copies, waits for them, and re-layouts  21.1 us (4%)
  between operations  14.2 us (3%)
  other arithmetic  10 us (2%)
    all_to_all x1, waiting for transfers between devices, body(): lax.all_to_all(jnp.stack([out_weight] * lax.axis_size(SUB)), SUB, 0, 0)  186 us
    reduce_scatter x3, waiting for transfers between devices, body(): partial = lax.psum_scatter(partial, axis, scatter_dimension=0, tiled=True)  93.6 us
    ppermute x6, waiting for transfers between devices, butterfly_sum(): lax.ppermute(value, axis, [(i, i ^ bit) for i in range(size)])  71.5 us
    ppermute x3, waiting for transfers between devices, scatter_ch(): lax.ppermute(block, 'ch', [(i, (i + k) % count) for i in range(count)])  44.9 us
    conv_general_dilated x3, matrix products, depthwise(): lax.conv_general_dilated(signal[None], kernel[:, None, :], (1,), 'VALID',...  31.8 us
    ppermute x3, waiting for transfers between devices, gather_ch(): lax.ppermute(part, 'ch', [(i, (i + k) % count) for i in range(count)])  24.5 us
    all_to_all x1, starting transfers between devices, body(): lax.all_to_all(jnp.stack([out_weight] * lax.axis_size(SUB)), SUB, 0, 0)  13.3 us
    ppermute x6, starting transfers between devices, butterfly_sum(): lax.ppermute(value, axis, [(i, i ^ bit) for i in range(size)])  12.5 us
  transfers between devices with their start and end apart: 18, of which 14 were waited for; matrix products, arithmetic and copies ran while one was open for 4% of the time, Pallas kernels for 0%

profile of v1, /device:TPU:1, one launch (start us, length us, event | category | flops | bytes accessed | tf_op | source)
XLA Modules:
  0.0 564.6 jit_solution(9298236279008608697)
XLA Ops:
  7.2 5.3 stack.17
  12.5 13.3 %all-to-all-start = ((bf16[64,64,1024]{2,1,0:T(8,128)(2,1)}), bf16[64,64,1024]{2,1,0:T(8,128)(2,1)}, u32[]{:S(2)}, u32[]{:S(2)}) async-start(bf16[64,64,1024]{2,1,0:T(8,128)(2,1)} %stack.17), calls=%async_computation | async-start | bytes 16777216 | tf_op jit(solution)/shard_map/all_to_all | solution.py:86
  25.9 185.6 %all-to-all-done = bf16[64,64,1024]{2,1,0:T(8,128)(2,1)} async-done(((bf16[64,64,1024]{2,1,0:T(8,128)(2,1)}), bf16[64,64,1024]{2,1,0:T(8,128)(2,1)}, u32[]{:S(2)}, u32[]{:S(2)}) %all-to-all-start) | async-done | bytes 8388640 | tf_op jit(solution)/shard_map/all_to_all | solution.py:86
  211.6 5.7 %fusion.27 = f32[256,4096]{1,0:T(8,128)S(1)} fusion(bf16[256,1024]{1,0:T(8,128)(2,1)S(1)} %copy-done, bf16[4096,1024]{1,0:T(8,128)(2,1)} %bitcast.12), kind=kOutput, calls=%fused_computation.51 | convolution fusion | flops 2147483648 | bytes 13107200 | tf_op jit(solution)/shard_map/dot_general | solution.py:91
  224.5 22.3 %collective-permute-done.4 = f32[256,1024]{1,0:T(8,128)S(1)} collective-permute-done((f32[256,1024]{1,0:T(8,128)}, f32[256,1024]{1,0:T(8,128)S(1)}, u32[]{:S(2)}, u32[]{:S(2)}) %collective-permute-start.4) | collective-permute-done | bytes 1048608 | tf_op jit(solution)/shard_map/ppermute | solution.py:57
  247.8 22.6 %collective-permute-done.5 = f32[256,1024]{1,0:T(8,128)} collective-permute-done((f32[256,1024]{1,0:T(8,128)}, f32[256,1024]{1,0:T(8,128)}, u32[]{:S(2)}, u32[]{:S(2)}) %collective-permute-start.5) | collective-permute-done | bytes 1048608 | tf_op jit(solution)/shard_map/ppermute | solution.py:57
  270.4 3.8 convert_multiply_fusion.3
  277.0 7.8 %collective-permute-done.7 = f32[127,1024]{1,0:T(8,128)} collective-permute-done((f32[127,1024]{1,0:T(8,128)S(1)}, f32[127,1024]{1,0:T(8,128)}, u32[]{:S(2)}, u32[]{:S(2)}) %collective-permute-start.7) | collective-permute-done | bytes 520224 | tf_op jit(solution)/shard_map/ppermute | solution.py:25
  286.0 10.6 %fusion.8 = f32[1,256,1024]{2,0,1:T(1,128)S(1)} fusion(f32[128,1,1024]{2,1,0:T(1,128)S(1)} %copy.20, f32[1,383,1024]{2,1,0:T(8,128)S(1)} %maximum_bitcast_fusion.1), kind=kOutput, calls=%fused_computation.12 | convolution fusion | flops 402653184 | bytes 3141632 | tf_op jit(solution)/shard_map/conv_general_dilated | solution.py:29
  303.6 10.6 %fusion.15 = f32[1,256,1024]{2,0,1:T(1,128)S(1)} fusion(f32[128,1,1024]{2,1,0:T(1,128)S(1)} %copy.18, bf16[1,383,1024]{2,1,0:T(8,128)(2,1)S(1)} %maximum_bitcast_fusion.2), kind=kOutput, calls=%fused_computation.22 | convolution fusion | flops 402653184 | bytes 2357248 | tf_op jit(solution)/shard_map/conv_general_dilated | solution.py:29
  317.9 11.5 %collective-permute-done.3 = bf16[256,1024]{1,0:T(8,128)(2,1)S(1)} collective-permute-done((bf16[256,1024]{1,0:T(8,128)(2,1)S(1)}, bf16[256,1024]{1,0:T(8,128)(2,1)S(1)}, u32[]{:S(2)}, u32[]{:S(2)}) %collective-permute-start.3) | collective-permute-done | bytes 524320 | tf_op jit(solution)/shard_map/ppermute | solution.py:44
  329.4 2.4 collective-permute-done.2
  331.8 10.6 %collective-permute-done.1 = bf16[256,1024]{1,0:T(8,128)(2,1)S(1)} collective-permute-done((bf16[256,1024]{1,0:T(8,128)(2,1)S(1)}, bf16[256,1024]{1,0:T(8,128)(2,1)S(1)}, u32[]{:S(2)}, u32[]{:S(2)}) %collective-permute-start.1) | collective-permute-done | bytes 524320 | tf_op jit(solution)/shard_map/ppermute | solution.py:44
  351.8 8.1 %fusion.28 = f32[4096,1024]{1,0:T(8,128)} fusion(bf16[256,4096]{0,1:T(8,128)(2,1)S(1)} %bitcast.51, bf16[256,1024]{1,0:T(8,128)(2,1)S(1)} %copy-done), kind=kOutput, calls=%fused_computation.52 | convolution fusion | flops 2147483648 | bytes 19398656 | tf_op jit(solution)/shard_map/dot_general | solution.py:108
  359.9 27.0 %reduce-scatter.4.cloned.1.call-done = f32[2048,1024]{1,0:T(8,128)} async-done(((f32[4096,1024]{1,0:T(8,128)}), f32[2048,1024]{1,0:T(8,128)}) %reduce-scatter.4.cloned.1.call-update) | async-done | bytes 8388624 | tf_op jit(solution)/shard_map/reduce_scatter | solution.py:112
  388.4 10.6 %fusion.13 = f32[1,128,1024]{2,0,1:T(1,128)S(1)} fusion(bf16[1,383,1024]{2,1,0:T(8,128)(2,1)S(1)} %copy-done.12, f32[256,1,1024]{2,0,1:T(8,128)S(1)} %bitcast.52), kind=kOutput, calls=%fused_computation.20 | convolution fusion | flops 402653184 | bytes 2357248 | tf_op jit(solution)/shard_map/conv_general_dilated | solution.py:29
  400.4 12.3 %collective-permute-done.8 = f32[1024,128]{0,1:T(8,128)S(1)} collective-permute-done((f32[1024,128]{0,1:T(8,128)S(1)}, f32[1024,128]{0,1:T(8,128)S(1)}, u32[]{:S(2)}, u32[]{:S(2)}) %collective-permute-start.8) | collective-permute-done | bytes 524320 | tf_op jit(solution)/shard_map/ppermute | solution.py:65
  412.8 2.6 collective-permute-start.9
  415.4 11.4 %collective-permute-done.9 = f32[1024,128]{0,1:T(8,128)S(1)} collective-permute-done((f32[1024,128]{0,1:T(8,128)S(1)}, f32[1024,128]{0,1:T(8,128)S(1)}, u32[]{:S(2)}, u32[]{:S(2)}) %collective-permute-start.9) | collective-permute-done | bytes 524320 | tf_op jit(solution)/shard_map/ppermute | solution.py:65
  427.9 66.6 %reduce-scatter.6.cloned.1.call-done = f32[256,1024]{1,0:T(8,128)} async-done(((f32[2048,1024]{1,0:T(8,128)}), f32[256,1024]{1,0:T(8,128)}) %reduce-scatter.6.cloned.1.call-update) | async-done | bytes 1048592 | tf_op jit(solution)/shard_map/reduce_scatter | solution.py:112
  497.1 23.5 %collective-permute-done.11 = f32[1024,128]{0,1:T(8,128)S(1)} collective-permute-done((f32[1024,128]{0,1:T(8,128)S(1)}, f32[1024,128]{0,1:T(8,128)S(1)}, u32[]{:S(2)}, u32[]{:S(2)}) %collective-permute-start.11) | collective-permute-done | bytes 524320 | tf_op jit(solution)/shard_map/ppermute | solution.py:65
  520.7 4.0 collective-permute-start.12
  524.7 24.3 %collective-permute-done.12 = f32[1024,128]{0,1:T(8,128)S(1)} collective-permute-done((f32[1024,128]{0,1:T(8,128)S(1)}, f32[1024,128]{0,1:T(8,128)S(1)}, u32[]{:S(2)}, u32[]{:S(2)}) %collective-permute-start.12) | collective-permute-done | bytes 524320 | tf_op jit(solution)/shard_map/ppermute | solution.py:65
  550.5 6.6 %fusion.10 = bf16[256,1024]{1,0:T(8,128)(2,1)} fusion(bf16[4096,1024]{1,0:T(8,128)(2,1)} %bitcast.12, bf16[256,1024]{1,0:T(8,128)(2,1)S(1)} %copy-done.18, bf16[256,1024]{1,0:T(8,128)(2,1)S(1)} %copy-done.17, bf16[256,1024]{1,0:T(8,128)(2,1)S(1)} %copy-done.16, bf16[256,1024]{1,0:T(8,128)(2,1)S(1)} %copy-done.15), kind=kOutput, calls=%fused_computation.19 | convolution fusion | flops 2156134400 | bytes 11010048 | tf_op jit(solution)/shard_map/dot_general | solution.py:88
  (91 shorter events, 41.2 us)
Async XLA Ops:
  7.2 204.4 %copy-start = (bf16[256,1024]{1,0:T(8,128)(2,1)S(1)}, bf16[256,1024]{1,0:T(8,128)(2,1)}, u32[]{:S(2)}) copy-start(bf16[256,1024]{1,0:T(8,128)(2,1)} %param.11) | copy-start | bytes 1572868
  12.5 199.1 %all-to-all-start = ((bf16[64,64,1024]{2,1,0:T(8,128)(2,1)}), bf16[64,64,1024]{2,1,0:T(8,128)(2,1)}, u32[]{:S(2)}, u32[]{:S(2)}) async-start(bf16[64,64,1024]{2,1,0:T(8,128)(2,1)} %stack.17), calls=%async_computation | async-start | bytes 16777216 | tf_op jit(solution)/shard_map/all_to_all | solution.py:86
  25.8 361.1 %reduce-scatter.4.cloned.1.call-start = ((), (), s32[]{:S(2)}) async-start(), calls=%async_computation.4 | async-start | bytes 25165824 | tf_op jit(solution)/shard_map/reduce_scatter | solution.py:112
  217.3 53.0 %copy-start.8 = (bf16[256,1024]{1,0:T(8,128)(2,1)S(1)}, bf16[256,1024]{1,0:T(8,128)(2,1)}, u32[]{:S(2)}) copy-start(bf16[256,1024]{1,0:T(8,128)(2,1)} %param.6) | copy-start | bytes 1572868
  220.2 26.6 %collective-permute-start.4 = (f32[256,1024]{1,0:T(8,128)}, f32[256,1024]{1,0:T(8,128)S(1)}, u32[]{:S(2)}, u32[]{:S(2)}) collective-permute-start(f32[256,1024]{1,0:T(8,128)} %get-tuple-element.20), channel_id=1, source_target_pairs={{0,1},{1,2},{2,3},{3,0},{4,5},{5,6},{6,7},{7,4},{8,9},{9,10},{10,1... | collective-permute-start | bytes 3145736 | tf_op jit(solution)/shard_map/ppermute | solution.py:57
  221.5 25.4 %collective-permute-start.6 = (f32[256,1024]{1,0:T(8,128)}, f32[256,1024]{1,0:T(8,128)}, u32[]{:S(2)}, u32[]{:S(2)}) collective-permute-start(f32[256,1024]{1,0:T(8,128)} %get-tuple-element.21), channel_id=1, source_target_pairs={{0,3},{1,0},{2,1},{3,2},{4,7},{5,4},{6,5},{7,6},{8,11},{9,8},{10,9... | collective-permute-start | bytes 3145736 | tf_op jit(solution)/shard_map/ppermute | solution.py:57
  222.9 47.5 %collective-permute-start.5 = (f32[256,1024]{1,0:T(8,128)}, f32[256,1024]{1,0:T(8,128)}, u32[]{:S(2)}, u32[]{:S(2)}) collective-permute-start(f32[256,1024]{1,0:T(8,128)} %get-tuple-element.22), channel_id=1, source_target_pairs={{0,2},{1,3},{2,0},{3,1},{4,6},{5,7},{6,4},{7,5},{8,10},{9,11},{10,... | collective-permute-start | bytes 3145736 | tf_op jit(solution)/shard_map/ppermute | solution.py:57
  274.2 10.6 %collective-permute-start.7 = (f32[127,1024]{1,0:T(8,128)S(1)}, f32[127,1024]{1,0:T(8,128)}, u32[]{:S(2)}, u32[]{:S(2)}) collective-permute-start(f32[127,1024]{1,0:T(8,128)S(1)} %slice.31), channel_id=1, source_target_pairs={{4,0},{8,4},{12,8},{16,12},{20,16},{24,20},{28,24},{32,28},{36,32}... | collective-permute-start | bytes 1560584 | tf_op jit(solution)/shard_map/ppermute | solution.py:25
  298.2 5.2 collective-permute-start
  315.5 13.9 %collective-permute-start.3 = (bf16[256,1024]{1,0:T(8,128)(2,1)S(1)}, bf16[256,1024]{1,0:T(8,128)(2,1)S(1)}, u32[]{:S(2)}, u32[]{:S(2)}) collective-permute-start(bf16[256,1024]{1,0:T(8,128)(2,1)S(1)} %get-tuple-element.35), channel_id=1, source_target_pairs={{0,3},{1,0},{2,1},{3,2},{4,7},{5,4},{6,5},{7,6},{8,11},{9,8},{10,9... | collective-permute-start | bytes 1572872 | tf_op jit(solution)/shard_map/ppermute | solution.py:44
  316.6 15.2 %collective-permute-start.2 = (bf16[256,1024]{1,0:T(8,128)(2,1)S(1)}, bf16[256,1024]{1,0:T(8,128)(2,1)S(1)}, u32[]{:S(2)}, u32[]{:S(2)}) collective-permute-start(bf16[256,1024]{1,0:T(8,128)(2,1)S(1)} %get-tuple-element.35), channel_id=1, source_target_pairs={{0,2},{1,3},{2,0},{3,1},{4,6},{5,7},{6,4},{7,5},{8,10},{9,11},{10,... | collective-permute-start | bytes 1572872 | tf_op jit(solution)/shard_map/ppermute | solution.py:44
  317.8 24.6 %collective-permute-start.1 = (bf16[256,1024]{1,0:T(8,128)(2,1)S(1)}, bf16[256,1024]{1,0:T(8,128)(2,1)S(1)}, u32[]{:S(2)}, u32[]{:S(2)}) collective-permute-start(bf16[256,1024]{1,0:T(8,128)(2,1)S(1)} %get-tuple-element.35), channel_id=1, source_target_pairs={{0,1},{1,2},{2,3},{3,0},{4,5},{5,6},{6,7},{7,4},{8,9},{9,10},{10,1... | collective-permute-start | bytes 1572872 | tf_op jit(solution)/shard_map/ppermute | solution.py:44
  359.9 134.7 %reduce-scatter.6.cloned.1.call-start = ((), (), s32[]{:S(2)}) async-start(), calls=%async_computation.5 | async-start | bytes 9437184 | tf_op jit(solution)/shard_map/reduce_scatter | solution.py:112
  387.0 171.1 %reduce-scatter.8.cloned.1.call-start = ((), (), s32[]{:S(2)}) async-start(), calls=%async_computation.6 | async-start | bytes 1310720 | tf_op jit(solution)/shard_map/reduce_scatter | solution.py:112
  399.4 13.3 %collective-permute-start.8 = (f32[1024,128]{0,1:T(8,128)S(1)}, f32[1024,128]{0,1:T(8,128)S(1)}, u32[]{:S(2)}, u32[]{:S(2)}) collective-permute-start(f32[1024,128]{0,1:T(8,128)S(1)} %bitcast.53), channel_id=1, source_target_pairs={{0,64},{64,0},{128,192},{192,128},{1,65},{65,1},{129,193},{193,129... | collective-permute-start | bytes 1572872 | tf_op jit(solution)/shard_map/ppermute | solution.py:65
  412.8 14.0 %collective-permute-start.9 = (f32[1024,128]{0,1:T(8,128)S(1)}, f32[1024,128]{0,1:T(8,128)S(1)}, u32[]{:S(2)}, u32[]{:S(2)}) collective-permute-start(f32[1024,128]{0,1:T(8,128)S(1)} %bitcast_add_fusion), channel_id=1, source_target_pairs={{0,128},{64,192},{128,0},{192,64},{1,129},{65,193},{129,1},{193,65... | collective-permute-start | bytes 1572872 | tf_op jit(solution)/shard_map/ppermute | solution.py:65
  426.8 67.8 %collective-permute-start.10 = (f32[1024,128]{0,1:T(8,128)S(1)}, f32[1024,128]{0,1:T(8,128)S(1)}, u32[]{:S(2)}, u32[]{:S(2)}) collective-permute-start(f32[1024,128]{0,1:T(8,128)S(1)} %add.103), channel_id=1, source_target_pairs={{0,8},{8,0},{16,24},{24,16},{32,40},{40,32},{48,56},{56,48},{1,9},... | collective-permute-start | bytes 1572872 | tf_op jit(solution)/shard_map/ppermute | solution.py:65
  494.6 55.8 %copy-start.15 = (bf16[256,1024]{1,0:T(8,128)(2,1)S(1)}, bf16[256,1024]{1,0:T(8,128)(2,1)}, u32[]{:S(2)}) copy-start(bf16[256,1024]{1,0:T(8,128)(2,1)} %get-tuple-element.24) | copy-start | bytes 1572868
  494.6 55.8 %copy-start.16 = (bf16[256,1024]{1,0:T(8,128)(2,1)S(1)}, bf16[256,1024]{1,0:T(8,128)(2,1)}, u32[]{:S(2)}) copy-start(bf16[256,1024]{1,0:T(8,128)(2,1)} %get-tuple-element.25) | copy-start | bytes 1572868
  494.6 55.8 %copy-start.17 = (bf16[256,1024]{1,0:T(8,128)(2,1)S(1)}, bf16[256,1024]{1,0:T(8,128)(2,1)}, u32[]{:S(2)}) copy-start(bf16[256,1024]{1,0:T(8,128)(2,1)} %get-tuple-element.26) | copy-start | bytes 1572868
  494.6 55.8 %copy-start.18 = (bf16[256,1024]{1,0:T(8,128)(2,1)S(1)}, bf16[256,1024]{1,0:T(8,128)(2,1)}, u32[]{:S(2)}) copy-start(bf16[256,1024]{1,0:T(8,128)(2,1)} %get-tuple-element.27) | copy-start | bytes 1572868
  494.7 25.9 %collective-permute-start.11 = (f32[1024,128]{0,1:T(8,128)S(1)}, f32[1024,128]{0,1:T(8,128)S(1)}, u32[]{:S(2)}, u32[]{:S(2)}) collective-permute-start(f32[1024,128]{0,1:T(8,128)S(1)} %add.104), channel_id=1, source_target_pairs={{0,16},{8,24},{16,0},{24,8},{32,48},{40,56},{48,32},{56,40},{1,17}... | collective-permute-start | bytes 1572872 | tf_op jit(solution)/shard_map/ppermute | solution.py:65
  520.7 28.3 %collective-permute-start.12 = (f32[1024,128]{0,1:T(8,128)S(1)}, f32[1024,128]{0,1:T(8,128)S(1)}, u32[]{:S(2)}, u32[]{:S(2)}) collective-permute-start(f32[1024,128]{0,1:T(8,128)S(1)} %add.105), channel_id=1, source_target_pairs={{0,32},{8,40},{16,48},{24,56},{32,0},{40,8},{48,16},{56,24},{1,33}... | collective-permute-start | bytes 1572872 | tf_op jit(solution)/shard_map/ppermute | solution.py:65
  549.0 8.0 %collective-permute-start.13 = (f32[1024,128]{0,1:T(8,128)S(1)}, f32[1024,128]{0,1:T(8,128)S(1)}, u32[]{:S(2)}, u32[]{:S(2)}) collective-permute-start(f32[1024,128]{0,1:T(8,128)S(1)} %add.106), channel_id=1, source_target_pairs={{0,4},{4,0},{1,5},{5,1},{2,6},{6,2},{3,7},{7,3},{8,12},{12,8},{9,1... | collective-permute-start | bytes 1572872 | tf_op jit(solution)/shard_map/ppermute | solution.py:65
  (13 other events, 129.7 us)
Sparse Core Ops, SparseCore 0:
  360.0 26.8 reduce-scatter.3
  389.5 105.0 reduce-scatter.5
  497.7 25.3 reduce-scatter.7
